TPU v7x, 256 devices: a whole 4x4x8 slice. The times are simulated.
256 devices in a mesh: dp: 8 (over x, core), expert: 32 (over y, z).
Axes of the slice: x: 4, y: 4, z: 8, core: 2. Of those that a mesh axis runs over, the one named last changes fastest.
Arguments:
- tokens: bfloat16 [4096, 3584], P('expert'), may hold values from -6 to 6
- cotangent: bfloat16 [4096, 3584], P('expert'), may hold values from -0.59765625 to 0.59765625
- route_ids: int32 [4096, 8], P('expert'), may hold values from 0 to 31, all different within a row; in each aligned block of 128 rows (0 to 127, 128 to 255, ...) at most 40 rows name the same one
- route_gates: float32 [4096, 8], P('expert'), may hold values from 0.02 to 0.5
- w_gate: bfloat16 [32, 1792, 3584], P('expert', 'dp'), may hold values from -0.09375 to 0.09375
- w_up: bfloat16 [32, 1792, 3584], P('expert', 'dp'), may hold values from -0.09375 to 0.09375
- w_down: bfloat16 [32, 1792, 3584], P('expert', 'dp'), may hold values from -0.125 to 0.125
Outputs:
- layer_out: bfloat16 [4096, 3584], P(('expert', 'dp'))
- gate_grad: float32 [4096, 8], P(('expert', 'dp'))
- grad_w_gate: bfloat16 [32, 1792, 3584], P('expert', 'dp')
- grad_w_up: bfloat16 [32, 1792, 3584], P('expert', 'dp')
- grad_w_down: bfloat16 [32, 1792, 3584], P('expert', 'dp')
Inputs may be any that keep to these rules, and one draw needn't show every extreme that they name: `route_ids`: each row names 8 different experts. Within each aligned block of 128 rows (the tokens of one index of expert) no expert is named more than 40 times, a bound that some block reaches.
All inputs are finite; a program needn't handle non-finite values.
Results may differ from a plain program's by a relative error of at most 0.02.
Values may be sent and summed in bfloat16 or wider, within the bound.
No kernel may reach another device: no remote copies, remote signals or barrier semaphores. Data moves between devices by JAX's collectives and lax.ppermute only.
A program may use at most 128 MiB of HBM per device.

v0:
```python
import jax
import jax.numpy as jnp
from jax import lax
from jax.sharding import PartitionSpec as P


def body(tokens, cotangent, route_ids, route_gates, w_gate, w_up, w_down):
    groups = lax.axis_size("expert")
    dp_count = lax.axis_size("dp")
    dp_idx = lax.axis_index("dp")
    tok_rows, width = tokens.shape
    top_slots = route_ids.shape[1]
    cap_rows = min(tok_rows, dp_count * max(1, tok_rows * top_slots * 5 // (4 * groups * dp_count)))
    share = cap_rows // dp_count
    n_dest = groups * share
    flat_ids = route_ids.reshape(-1)
    onehot = (flat_ids[:, None] == jnp.arange(groups, dtype=jnp.int32)[None, :]).astype(jnp.int32)
    n_slots = flat_ids.shape[0]
    lower = (
        jnp.arange(n_slots, dtype=jnp.int32)[:, None]
        >= jnp.arange(n_slots, dtype=jnp.int32)[None, :]
    ).astype(jnp.bfloat16)
    running = jnp.dot(lower, onehot.astype(jnp.bfloat16), preferred_element_type=jnp.float32)
    slot_rank = jnp.sum(running.astype(jnp.int32) * onehot, axis=1) - 1
    local_rank = slot_rank - dp_idx * share
    mine = (local_rank >= 0) & (local_rank < share)
    dest = jnp.where(mine, local_rank * groups + flat_ids, n_dest)
    dest_hot = (dest[:, None] == jnp.arange(n_dest, dtype=jnp.int32)[None, :]).astype(jnp.float32)
    pick = jnp.sum(dest_hot.reshape(tok_rows, top_slots, n_dest), axis=1).T
    pick_bf = pick.astype(jnp.bfloat16)
    gate_sel = jnp.sum(dest_hot * route_gates.reshape(-1)[:, None], axis=0)
    send_x = jnp.dot(pick_bf, tokens, preferred_element_type=jnp.float32).astype(jnp.bfloat16)
    cot_sel = jnp.dot(pick_bf, cotangent, preferred_element_type=jnp.float32)
    send_dy = (gate_sel[:, None] * cot_sel).astype(jnp.bfloat16)

    def to_lanes(rows):
        return jnp.concatenate([rows[r * groups : (r + 1) * groups] for r in range(share)], axis=1)

    def lanes_to_rows(packed):
        return jnp.concatenate(
            [packed[:, r * width : (r + 1) * width] for r in range(share)], axis=0
        )

    recv_x = lax.all_to_all(to_lanes(send_x), "expert", split_axis=0, concat_axis=0, tiled=True)
    recv_x, lanes_dy = lax.optimization_barrier((recv_x, to_lanes(send_dy)))
    recv_dy = lax.all_to_all(lanes_dy, "expert", split_axis=0, concat_axis=0, tiled=True)
    gathered_x = lax.all_gather(recv_x, "dp", axis=0, tiled=True)
    x_chunks = [gathered_x[:, r * width : (r + 1) * width] for r in range(share)]
    gate_local = w_gate[0]
    up_local = w_up[0]
    down_local = w_down[0]
    by_feature = (((1,), (1,)), ((), ()))
    by_row = (((0,), (0,)), ((), ()))
    gate_pre = jnp.concatenate(
        [
            lax.dot_general(xc, gate_local, by_feature, preferred_element_type=jnp.float32)
            for xc in x_chunks
        ],
        axis=0,
    )
    up_pre = jnp.concatenate(
        [
            lax.dot_general(xc, up_local, by_feature, preferred_element_type=jnp.float32)
            for xc in x_chunks
        ],
        axis=0,
    )
    sigma_gate = jax.nn.sigmoid(gate_pre)
    hidden = (gate_pre * sigma_gate * up_pre).astype(jnp.bfloat16)
    stack_rows = dp_count * groups
    y_lanes = jnp.concatenate(
        [
            jnp.dot(
                hidden[r * stack_rows : (r + 1) * stack_rows],
                down_local,
                preferred_element_type=jnp.float32,
            ).astype(jnp.bfloat16)
            for r in range(share)
        ],
        axis=1,
    )
    flat_x = jnp.concatenate(x_chunks, axis=0)
    y_sum = lax.psum_scatter(y_lanes, "dp", scatter_dimension=0, tiled=True)
    y_sum, recv_dy = lax.optimization_barrier((y_sum, recv_dy))
    flat_dy = lanes_to_rows(lax.all_gather(recv_dy, "dp", axis=0, tiled=True))
    y_back = lax.all_to_all(y_sum, "expert", split_axis=0, concat_axis=0, tiled=True)
    y_back, flat_dy = lax.optimization_barrier((y_back, flat_dy))
    y_home = lanes_to_rows(y_back).astype(jnp.float32)
    hidden_grad = lax.dot_general(
        flat_dy, down_local, by_feature, preferred_element_type=jnp.float32
    )
    grad_gate_pre = (
        hidden_grad * up_pre * sigma_gate * (1.0 + gate_pre * (1.0 - sigma_gate))
    ).astype(jnp.bfloat16)
    grad_up_pre = (hidden_grad * gate_pre * sigma_gate).astype(jnp.bfloat16)
    grad_down = lax.dot_general(hidden, flat_dy, by_row, preferred_element_type=jnp.float32)
    grad_gate = lax.dot_general(grad_gate_pre, flat_x, by_row, preferred_element_type=jnp.float32)
    grad_up = lax.dot_general(grad_up_pre, flat_x, by_row, preferred_element_type=jnp.float32)
    out_part = lax.dot_general(
        pick,
        gate_sel[:, None] * y_home,
        by_row,
        precision=lax.Precision.HIGHEST,
        preferred_element_type=jnp.float32,
    )
    dot_dest = jnp.sum(cot_sel * y_home, axis=1)
    grad_part = jnp.sum(dest_hot * dot_dest[None, :], axis=1).reshape(tok_rows, top_slots)
    both_sum = lax.psum_scatter(
        jnp.concatenate([out_part, grad_part], axis=1).astype(jnp.bfloat16),
        "dp",
        scatter_dimension=0,
        tiled=True,
    )
    layer_sum = both_sum[:, :width]
    gate_sum = both_sum[:, width:].astype(jnp.float32)
    return (
        layer_sum.astype(jnp.bfloat16),
        gate_sum,
        grad_gate.astype(jnp.bfloat16)[None],
        grad_up.astype(jnp.bfloat16)[None],
        grad_down.astype(jnp.bfloat16)[None],
    )


def solution(mesh):
    return jax.shard_map(
        body,
        mesh=mesh,
        in_specs=(
            P("expert", None),
            P("expert", None),
            P("expert", None),
            P("expert", None),
            P("expert", "dp", None),
            P("expert", "dp", None),
            P("expert", "dp", None),
        ),
        out_specs=(
            P(("expert", "dp"), None),
            P(("expert", "dp"), None),
            P("expert", "dp", None),
            P("expert", "dp", None),
            P("expert", "dp", None),
        ),
        check_vma=False,
    )
```

profile of v0, /device:TPU:8, one launch (start us, length us, event | category | flops | bytes accessed | tf_op | source)
XLA Modules:
  0.0 315.9 jit_solution(5336384310232286521)
XLA Ops:
  11.3 2.8 reduce
  14.0 1.2 reshape.61
  15.2 11.8 %all-to-all-start = ((bf16[32,2,8960]{2,1,0:T(2,128)(2,1)}), bf16[32,2,8960]{2,1,0:T(2,128)(2,1)S(1)}, u32[]{:S(2)}, u32[]{:S(2)}) async-start(bf16[32,2,8960]{2,1,0:T(2,128)(2,1)} %reshape.61), calls=%async_computation | async-start | bytes 2293760 | tf_op jit(solution)/shard_map/all_to_all | solution.py:44
  27.4 3.0 multiply_convert_fusion
  34.0 21.2 %all-to-all-done = bf16[32,2,8960]{2,1,0:T(2,128)(2,1)S(1)} async-done(((bf16[32,2,8960]{2,1,0:T(2,128)(2,1)}), bf16[32,2,8960]{2,1,0:T(2,128)(2,1)S(1)}, u32[]{:S(2)}, u32[]{:S(2)}) %all-to-all-start) | async-done | bytes 1146912 | tf_op jit(solution)/shard_map/all_to_all | solution.py:44
  55.1 3.4 %reshape.62 = bf16[32,1,17920]{2,1,0:T(2,128)(2,1)} reshape(bf16[32,2,8960]{2,1,0:T(2,128)(2,1)S(1)} %all-to-all-done) | data formatting | bytes 2293760
  58.6 2.9 copy.48
  61.5 54.5 %all-gather.3.cloned.1.call-done = bf16[256,17920]{1,0:T(8,128)(2,1)} async-done(((bf16[32,17920]{1,0:T(8,128)(2,1)}), bf16[256,17920]{1,0:T(8,128)(2,1)}) %all-gather.3.cloned.1.call-update) | async-done | bytes 9175056 | tf_op jit(solution)/shard_map/all_gather | solution.py:47
  116.0 2.4 fusion.72
  118.4 2.7 fusion.77
  121.1 2.2 fusion.82
  129.4 1.9 fusion.4
  131.3 1.9 fusion.3
  133.2 1.9 fusion.2
  135.1 1.9 fusion.1
  137.1 2.0 fusion
  139.1 2.8 reduce.1
  141.9 1.2 reshape.63
  143.0 41.6 %all_to_all.36 = bf16[32,2,8960]{2,1,0:T(2,128)(2,1)S(1)} all-to-all(bf16[32,2,8960]{2,1,0:T(2,128)(2,1)} %reshape.63), channel_id=1, replica_groups=mesh['dp'=8,'expert'=32] {'expert'}, dimensions={0} | all-to-all | bytes 2293760 | tf_op jit(solution)/shard_map/all_to_all | solution.py:46
  184.6 3.4 %reshape.64 = bf16[32,1,17920]{2,1,0:T(2,128)(2,1)} reshape(bf16[32,2,8960]{2,1,0:T(2,128)(2,1)S(1)} %all_to_all.36) | data formatting | bytes 2293760
  188.0 2.9 copy.47
  190.9 7.3 %reduce-scatter.3.cloned.1.call-done = bf16[32,17920]{1,0:T(8,128)(2,1)} async-done(((bf16[256,17920]{1,0:T(8,128)(2,1)}), bf16[32,17920]{1,0:T(8,128)(2,1)}) %reduce-scatter.3.cloned.1.call-update) | async-done | bytes 1146896 | tf_op jit(solution)/shard_map/reduce_scatter | solution.py:83
  198.2 1.6 slice_dynamic-update-slice_fusion.9
  199.8 1.6 slice_dynamic-update-slice_fusion.8
  201.5 3.6 %copy-done.9 = bf16[1280,3584]{1,0:T(8,128)(2,1)} copy-done((bf16[1280,3584]{1,0:T(8,128)(2,1)}, bf16[1280,3584]{1,0:T(8,128)(2,1)S(1)}, u32[]{:S(2)}) %copy-start.9) | copy-done | bytes 9175064
  205.1 2.8 reduce.2
  207.9 1.2 reshape.65
  209.0 10.1 %all-to-all-start.2 = ((bf16[32,2,8960]{2,1,0:T(2,128)(2,1)}), bf16[32,2,8960]{2,1,0:T(2,128)(2,1)S(1)}, u32[]{:S(2)}, u32[]{:S(2)}) async-start(bf16[32,2,8960]{2,1,0:T(2,128)(2,1)} %reshape.65), calls=%async_computation.3 | async-start | bytes 2293760 | tf_op jit(solution)/shard_map/all_to_all | solution.py:86
  219.2 2.9 slice_dynamic-update-slice_fusion.7
  222.1 3.0 slice_dynamic-update-slice_fusion.6
  225.1 2.9 slice_dynamic-update-slice_fusion.5
  228.0 18.9 %all-to-all-done.2 = bf16[32,2,8960]{2,1,0:T(2,128)(2,1)S(1)} async-done(((bf16[32,2,8960]{2,1,0:T(2,128)(2,1)}), bf16[32,2,8960]{2,1,0:T(2,128)(2,1)S(1)}, u32[]{:S(2)}, u32[]{:S(2)}) %all-to-all-start.2) | async-done | bytes 1146912 | tf_op jit(solution)/shard_map/all_to_all | solution.py:86
  247.0 3.4 %reshape.66 = bf16[32,1,17920]{2,1,0:T(2,128)(2,1)} reshape(bf16[32,2,8960]{2,1,0:T(2,128)(2,1)S(1)} %all-to-all-done.2) | data formatting | bytes 2293760
  250.4 1.8 copy.46
  252.1 3.6 %all-gather.5.cloned.1.call-done = bf16[256,17920]{1,0:T(8,128)(2,1)} async-done(((bf16[32,17920]{1,0:T(8,128)(2,1)}), bf16[256,17920]{1,0:T(8,128)(2,1)}) %all-gather.5.cloned.1.call-update) | async-done | bytes 9175056 | tf_op jit(solution)/shard_map/all_gather | solution.py:85
  255.8 1.6 slice_dynamic-update-slice_fusion.4
  257.4 1.6 slice_dynamic-update-slice_fusion.3
  259.0 1.6 slice_dynamic-update-slice_fusion.2
  260.6 1.6 slice_dynamic-update-slice_fusion.1
  262.3 1.6 slice_dynamic-update-slice_fusion
  263.9 4.0 %fusion.10 = f32[1280,224]{0,1:T(8,128)} fusion(bf16[1280,3584]{1,0:T(8,128)(2,1)S(1)} %slice_dynamic-update-slice_fusion, bf16[1,224,3584]{2,1,0:T(8,128)(2,1)S(1)} %copy-done), kind=kOutput, calls=%fused_computation.29 | convolution fusion | flops 2055208960 | bytes 11927552 | tf_op jit(solution)/shard_map/dot_general | solution.py:89
  268.0 1.9 convolution_convert_fusion.9
  270.5 1.0 pad_maximum_fusion
  271.6 7.2 %fusion.7 = bf16[1,224,3584]{2,1,0:T(8,128)(2,1)} fusion(bf16[1280,224]{0,1:T(8,128)(2,1)S(1)} %multiply_convert_fusion.3, bf16[1280,3584]{1,0:T(8,128)(2,1)} %copy-done.10), kind=kOutput, calls=%fused_computation.16 | convolution fusion | flops 2056011776 | bytes 11354112 | tf_op jit(solution)/shard_map/dot_general | solution.py:96
  278.8 3.5 %fusion.6 = bf16[1,224,3584]{2,1,0:T(8,128)(2,1)} fusion(bf16[1280,3584]{1,0:T(8,128)(2,1)S(1)} %bitcast.91, f32[1280,224]{0,1:T(8,128)S(1)} %copy-done.14, f32[1280,224]{0,1:T(8,128)S(1)} %copy-done.7), kind=kOutput, calls=%fused_computation.15 | convolution fusion | flops 2057732096 | bytes 13074432 | tf_op jit(solution)/shard_map/dot_general | solution.py:98
  282.3 3.7 %fusion.5 = bf16[1,224,3584]{2,1,0:T(8,128)(2,1)} fusion(bf16[1280,3584]{1,0:T(8,128)(2,1)S(1)} %bitcast.91, f32[1280,224]{0,1:T(8,128)S(1)} %copy-done.7, f32[1280,224]{0,1:T(8,128)S(1)} %copy-done.14, f32[1280,224]{0,1:T(8,128)S(1)} %copy-done.5), kind=kOutput, calls=%fused_computation.14 | convolution fusion | flops 2058878976 | bytes 14221312 | tf_op jit(solution)/shard_map/dot_general | solution.py:97
  286.0 20.5 %reduce-scatter.5.cloned.1.call-done = bf16[16,3592]{1,0:T(8,128)(2,1)} async-done(((bf16[128,3592]{1,0:T(8,128)(2,1)}), bf16[16,3592]{1,0:T(8,128)(2,1)}) %reduce-scatter.5.cloned.1.call-update) | async-done | bytes 114960 | tf_op jit(solution)/shard_map/reduce_scatter | solution.py:108
  307.8 1.6 slice.153
  (86 shorter events, 16.1 us)
Async XLA Ops:
  7.2 122.2 %copy-start = (bf16[1,224,3584]{2,1,0:T(8,128)(2,1)S(1)}, bf16[1,224,3584]{2,1,0:T(8,128)(2,1)}, u32[]{:S(2)}) copy-start(bf16[1,224,3584]{2,1,0:T(8,128)(2,1)} %param.13) | copy-start | bytes 4816900
  7.2 2.0 copy-start.8
  9.7 1.0 copy-start.3
  15.2 11.9 %copy-start.11 = (f32[128,8]{0,1:T(8,128)S(1)}, f32[128,8]{0,1:T(8,128)}, u32[]{:S(2)}) copy-start(f32[128,8]{0,1:T(8,128)} %param.10) | copy-start | bytes 12292
  15.2 40.0 %all-to-all-start = ((bf16[32,2,8960]{2,1,0:T(2,128)(2,1)}), bf16[32,2,8960]{2,1,0:T(2,128)(2,1)S(1)}, u32[]{:S(2)}, u32[]{:S(2)}) async-start(bf16[32,2,8960]{2,1,0:T(2,128)(2,1)} %reshape.61), calls=%async_computation | async-start | bytes 2293760 | tf_op jit(solution)/shard_map/all_to_all | solution.py:44
  27.0 89.0 %all-gather.3.cloned.1.call-start = ((), (), s32[]{:S(2)}) async-start(), calls=%async_computation.5 | async-start | bytes 10321920 | tf_op jit(solution)/shard_map/all_gather | solution.py:47
  58.6 57.4 %copy-start.12 = (bf16[1,224,3584]{2,1,0:T(8,128)(2,1)S(1)}, bf16[1,224,3584]{2,1,0:T(8,128)(2,1)}, u32[]{:S(2)}) copy-start(bf16[1,224,3584]{2,1,0:T(8,128)(2,1)} %param.12) | copy-start | bytes 4816900
  61.5 136.7 %reduce-scatter.3.cloned.1.call-start = ((), (), s32[]{:S(2)}) async-start(), calls=%async_computation.6 | async-start | bytes 10321920 | tf_op jit(solution)/shard_map/reduce_scatter | solution.py:83
  116.0 7.3 %copy-start.1 = (bf16[256,17920]{1,0:T(8,128)(2,1)S(1)}, bf16[256,17920]{1,0:T(8,128)(2,1)}, u32[]{:S(2)}) copy-start(bf16[256,17920]{1,0:T(8,128)(2,1)} %all-gather.3.cloned.1.call-done) | copy-start | bytes 27525124
  124.0 1.4 copy-start.13
  125.5 3.6 %copy-start.4 = (f32[1280,224]{0,1:T(8,128)}, f32[1280,224]{0,1:T(8,128)S(1)}, u32[]{:S(2)}) copy-start(f32[1280,224]{0,1:T(8,128)S(1)} %fusion.92) | copy-start | bytes 3440644
  129.0 2.3 copy-start.6
  139.0 116.7 %all-gather.5.cloned.1.call-start = ((), (), s32[]{:S(2)}) async-start(), calls=%async_computation.7 | async-start | bytes 10321920 | tf_op jit(solution)/shard_map/all_gather | solution.py:85
  201.5 3.6 %copy-start.9 = (bf16[1280,3584]{1,0:T(8,128)(2,1)}, bf16[1280,3584]{1,0:T(8,128)(2,1)S(1)}, u32[]{:S(2)}) copy-start(bf16[1280,3584]{1,0:T(8,128)(2,1)S(1)} %slice_dynamic-update-slice_fusion.8) | copy-start | bytes 27525124
  209.0 37.9 %all-to-all-start.2 = ((bf16[32,2,8960]{2,1,0:T(2,128)(2,1)}), bf16[32,2,8960]{2,1,0:T(2,128)(2,1)S(1)}, u32[]{:S(2)}, u32[]{:S(2)}) async-start(bf16[32,2,8960]{2,1,0:T(2,128)(2,1)} %reshape.65), calls=%async_computation.3 | async-start | bytes 2293760 | tf_op jit(solution)/shard_map/all_to_all | solution.py:86
  219.2 87.3 %reduce-scatter.5.cloned.1.call-start = ((), (), s32[]{:S(2)}) async-start(), calls=%async_computation.8 | async-start | bytes 1069056 | tf_op jit(solution)/shard_map/reduce_scatter | solution.py:108
  263.9 4.0 %copy-start.10 = (bf16[1280,3584]{1,0:T(8,128)(2,1)}, bf16[1280,3584]{1,0:T(8,128)(2,1)S(1)}, u32[]{:S(2)}) copy-start(bf16[1280,3584]{1,0:T(8,128)(2,1)S(1)} %slice_dynamic-update-slice_fusion) | copy-start | bytes 27525124
  268.0 1.9 copy-start.2
  271.5 7.2 %slice-start = ((s8[9175040]{0:T(1024)(128)(4,1)}), s8[786432]{0:T(1024)(128)(4,1)S(1)}, s32[]{:S(2)}) async-start(s8[9175040]{0:T(1024)(128)(4,1)} %bitcast.90), calls=%async_computation.9 | async-start | bytes 1572864
  271.5 7.2 %copy-start.7 = (f32[1280,224]{0,1:T(8,128)S(1)}, f32[1280,224]{0,1:T(8,128)}, u32[]{:S(2)}) copy-start(f32[1280,224]{0,1:T(8,128)} %copy-done.6) | copy-start | bytes 3440644
  271.6 7.2 %slice-start.1 = ((s8[9175040]{0:T(1024)(128)(4,1)}), s8[4194304]{0:T(1024)(128)(4,1)S(1)}, s32[]{:S(2)}) async-start(s8[9175040]{0:T(1024)(128)(4,1)} %bitcast.90), calls=%async_computation.10 | async-start | bytes 8388608
  271.6 7.2 %slice-start.2 = ((s8[9175040]{0:T(1024)(128)(4,1)}), s8[4194304]{0:T(1024)(128)(4,1)S(1)}, s32[]{:S(2)}) async-start(s8[9175040]{0:T(1024)(128)(4,1)} %bitcast.90), calls=%async_computation.11 | async-start | bytes 8388608
  271.6 7.2 %copy-start.14 = (f32[1280,224]{0,1:T(8,128)S(1)}, f32[1280,224]{0,1:T(8,128)}, u32[]{:S(2)}) copy-start(f32[1280,224]{0,1:T(8,128)} %fusion.10) | copy-start | bytes 3440644
  278.8 3.5 %copy-start.5 = (f32[1280,224]{0,1:T(8,128)S(1)}, f32[1280,224]{0,1:T(8,128)}, u32[]{:S(2)}) copy-start(f32[1280,224]{0,1:T(8,128)} %copy-done.4) | copy-start | bytes 3440644
Sparse Core Ops, SparseCore 0:
  61.6 54.3 all-gather.2
  139.2 58.9 reduce-scatter.2
  200.6 55.1 all-gather.4
  271.7 34.7 reduce-scatter.4
where the time goes:
time: 317 us; the launch traced here: 316 us
  waiting for transfers between devices  126 us (40%)
  local copies, waits for them, and re-layouts  54.7 us (17%)
  matrix products  46.1 us (15%)
  blocking collectives  41.6 us (13%)
  starting transfers between devices  22.1 us (7%)
  between operations  14.3 us (5%)
  other arithmetic  11.1 us (4%)
    all_gather x1, waiting for transfers between devices, body(): gathered_x = lax.all_gather(recv_x, 'dp', axis=0, tiled=True)  54.5 us
    unnamed x68, local copies, waits for them, and re-layouts  46.8 us
    all_to_all x1, blocking collectives, body(): lax.all_to_all(lanes_dy, 'expert', split_axis=0, concat_axis=0, tiled=True)  41.6 us
    all_to_all x1, waiting for transfers between devices, body(): lax.all_to_all(to_lanes(send_x), 'expert', split_axis=0, concat_axis=0, t...  21.2 us
    reduce_scatter x1, waiting for transfers between devices, body(): lax.psum_scatter(jnp.concatenate([out_part, grad_part], axis=1).astype(jn...  20.5 us
    all_to_all x1, waiting for transfers between devices, body(): lax.all_to_all(y_sum, 'expert', split_axis=0, concat_axis=0, tiled=True)  18.9 us
    all_to_all x1, starting transfers between devices, body(): lax.all_to_all(to_lanes(send_x), 'expert', split_axis=0, concat_axis=0, t...  11.8 us
    all_to_all x1, starting transfers between devices, body(): lax.all_to_all(y_sum, 'expert', split_axis=0, concat_axis=0, tiled=True)  10.1 us
  transfers between devices with their start and end apart: 6, of which 6 were waited for; matrix products, arithmetic and copies ran while one was open for 17% of the time, Pallas kernels for 0%

commit v1 on v0

--- a/solution.py
+++ b/solution.py
@@ -2,6 +2,12 @@
 import jax.numpy as jnp
 from jax import lax
 from jax.sharding import PartitionSpec as P
+
+
+def joined_along(blocks, dim):
+    dims = list(blocks.shape[1:])
+    dims[dim] *= blocks.shape[0]
+    return jnp.moveaxis(blocks, 0, dim).reshape(dims)
 
 
 def body(tokens, cotangent, route_ids, route_gates, w_gate, w_up, w_down):
@@ -44,7 +50,19 @@
     recv_x = lax.all_to_all(to_lanes(send_x), "expert", split_axis=0, concat_axis=0, tiled=True)
     recv_x, lanes_dy = lax.optimization_barrier((recv_x, to_lanes(send_dy)))
     recv_dy = lax.all_to_all(lanes_dy, "expert", split_axis=0, concat_axis=0, tiled=True)
-    gathered_x = lax.all_gather(recv_x, "dp", axis=0, tiled=True)
+    size = lax.axis_size("dp")
+    pairs = [(i, (i + 1) % size) for i in range(size)]
+    back = [(b, a) for a, b in pairs]
+    lower_2, upper = ([], [])
+    for hop in range(size - 1):
+        if hop % 2 == 0:
+            lower_2.append(lax.ppermute(lower_2[-1] if lower_2 else recv_x, "dp", pairs))
+        else:
+            upper.append(lax.ppermute(upper[-1] if upper else recv_x, "dp", back))
+    blocks = jnp.stack([*lower_2[::-1], recv_x, *upper])
+    shift = lax.axis_index("dp") - len(lower_2)
+    blocks = blocks[(jnp.arange(size) - shift) % size]
+    gathered_x = joined_along(blocks, 0)
     x_chunks = [gathered_x[:, r * width : (r + 1) * width] for r in range(share)]
     gate_local = w_gate[0]
     up_local = w_up[0]

time: 317 us -> 349 us (1.10)
  local copies, waits for them, and re-layouts: 54.7 us -> 76.6 us
  starting transfers between devices: 22.1 us -> 31.4 us
  blocking collectives: 41.6 us -> 33.3 us
  waiting for transfers between devices: 126 us -> 133 us
    ppermute x0 -> x7, waiting for transfers between devices: none -> 57.2 us  [the longest x4 57.1 us: body(): lax.ppermute(lower_2[-1] if lower_2 else recv_x, 'dp', pairs)]
    all_gather x1 -> x0, waiting for transfers between devices: 54.5 us -> none  [body(): gathered_x = lax.all_gather(recv_x, 'dp', axis=0, tiled=True)]
    unnamed x68 -> x83, local copies, waits for them, and re-layouts: 46.8 us -> 59 us
    ppermute x0 -> x7, starting transfers between devices: none -> 9.14 us  [the longest x3 9.11 us: body(): upper.append(lax.ppermute(upper[-1] if upper else recv_x, 'dp', back))]
    gather x0 -> x1, local copies, waits for them, and re-layouts: none -> 8.68 us  [body(): blocks = blocks[(jnp.arange(size) - shift) % size]]
    all_to_all x1, blocking collectives: 41.6 us -> 33.3 us  [body(): lax.all_to_all(lanes_dy, 'expert', split_axis=0, concat_axis=0, tiled=True)]
    reduce_scatter x1, waiting for transfers between devices: 7.35 us -> 11.6 us  [body(): y_sum = lax.psum_scatter(y_lanes, 'dp', scatter_dimension=0, tiled=True)]
  transfers between devices with their start and end apart: 6 -> 12, of which waited for: 6 -> 10; matrix products, arithmetic and copies ran while one was open for 17% -> 19% of each run, Pallas kernels for 0% -> 0%
where the time goes in v1:
time: 349 us; the launch traced here: 348 us
  waiting for transfers between devices  133 us (38%)
  local copies, waits for them, and re-layouts  76.6 us (22%)
  matrix products  47.7 us (14%)
  blocking collectives  33.3 us (10%)
  starting transfers between devices  31.4 us (9%)
  between operations  14.3 us (4%)
  other arithmetic  11.1 us (3%)
    unnamed x83, local copies, waits for them, and re-layouts  59 us
    ppermute x4, waiting for transfers between devices, body(): lax.ppermute(lower_2[-1] if lower_2 else recv_x, 'dp', pairs)  57.1 us
    all_to_all x1, blocking collectives, body(): lax.all_to_all(lanes_dy, 'expert', split_axis=0, concat_axis=0, tiled=True)  33.3 us
    all_to_all x1, waiting for transfers between devices, body(): lax.all_to_all(to_lanes(send_x), 'expert', split_axis=0, concat_axis=0, t...  21.1 us
    reduce_scatter x1, waiting for transfers between devices, body(): lax.psum_scatter(jnp.concatenate([out_part, grad_part], axis=1).astype(jn...  20.5 us
    all_to_all x1, waiting for transfers between devices, body(): lax.all_to_all(y_sum, 'expert', split_axis=0, concat_axis=0, tiled=True)  18.9 us
    all_to_all x1, starting transfers between devices, body(): lax.all_to_all(to_lanes(send_x), 'expert', split_axis=0, concat_axis=0, t...  11.8 us
    reduce_scatter x1, waiting for transfers between devices, body(): y_sum = lax.psum_scatter(y_lanes, 'dp', scatter_dimension=0, tiled=True)  11.6 us
  transfers between devices with their start and end apart: 12, of which 10 were waited for; matrix products, arithmetic and copies ran while one was open for 19% of the time, Pallas kernels for 0%

profile of v1, /device:TPU:8, one launch (start us, length us, event | category | flops | bytes accessed | tf_op | source)
XLA Modules:
  0.0 347.5 jit_solution(1816224620301165280)
XLA Ops:
  11.3 2.8 reduce
  15.2 11.8 %all-to-all-start = ((bf16[32,2,8960]{2,1,0:T(2,128)(2,1)}), bf16[32,2,8960]{2,1,0:T(2,128)(2,1)S(1)}, u32[]{:S(2)}, u32[]{:S(2)}) async-start(bf16[32,2,8960]{2,1,0:T(2,128)(2,1)} %reshape.122), calls=%async_computation | async-start | bytes 2293760 | tf_op jit(solution)/shard_map/all_to_all | solution.py:50
  27.4 3.1 multiply_convert_fusion
  34.0 21.1 %all-to-all-done = bf16[32,2,8960]{2,1,0:T(2,128)(2,1)S(1)} async-done(((bf16[32,2,8960]{2,1,0:T(2,128)(2,1)}), bf16[32,2,8960]{2,1,0:T(2,128)(2,1)S(1)}, u32[]{:S(2)}, u32[]{:S(2)}) %all-to-all-start) | async-done | bytes 1146912 | tf_op jit(solution)/shard_map/all_to_all | solution.py:50
  55.1 3.4 reshape.123
  58.5 1.8 copy.48
  60.3 16.5 %collective-permute-done = bf16[32,17920]{1,0:T(8,128)(2,1)S(1)} collective-permute-done((bf16[32,17920]{1,0:T(8,128)(2,1)S(1)}, bf16[32,17920]{1,0:T(8,128)(2,1)S(1)}, u32[]{:S(2)}, u32[]{:S(2)}) %collective-permute-start) | collective-permute-done | bytes 1146912 | tf_op jit(solution)/shard_map/ppermute | solution.py:59
  76.8 3.0 collective-permute-start.4
  79.8 13.5 %collective-permute-done.1 = bf16[32,17920]{1,0:T(8,128)(2,1)S(1)} collective-permute-done((bf16[32,17920]{1,0:T(8,128)(2,1)S(1)}, bf16[32,17920]{1,0:T(8,128)(2,1)S(1)}, u32[]{:S(2)}, u32[]{:S(2)}) %collective-permute-start.1) | collective-permute-done | bytes 1146912 | tf_op jit(solution)/shard_map/ppermute | solution.py:59
  93.3 3.0 collective-permute-start.5
  96.4 13.5 %collective-permute-done.2 = bf16[32,17920]{1,0:T(8,128)(2,1)} collective-permute-done((bf16[32,17920]{1,0:T(8,128)(2,1)S(1)}, bf16[32,17920]{1,0:T(8,128)(2,1)}, u32[]{:S(2)}, u32[]{:S(2)}) %collective-permute-start.2) | collective-permute-done | bytes 1146912 | tf_op jit(solution)/shard_map/ppermute | solution.py:59
  110.0 3.1 collective-permute-start.6
  113.2 13.5 %collective-permute-done.3 = bf16[32,17920]{1,0:T(8,128)(2,1)} collective-permute-done((bf16[32,17920]{1,0:T(8,128)(2,1)}, bf16[32,17920]{1,0:T(8,128)(2,1)}, u32[]{:S(2)}, u32[]{:S(2)}) %collective-permute-start.3) | collective-permute-done | bytes 1146912 | tf_op jit(solution)/shard_map/ppermute | solution.py:59
  126.7 2.3 bitcast_dynamic-update-slice_fusion.7
  129.0 2.4 bitcast_dynamic-update-slice_fusion.6
  135.4 2.4 bitcast_dynamic-update-slice_fusion.2
  137.7 2.3 bitcast_dynamic-update-slice_fusion.1
  141.2 8.7 %gather_fusion = bf16[8,32,17920]{2,1,0:T(8,128)(2,1)} fusion(bf16[8,32,17920]{2,1,0:T(8,128)(2,1)} %bitcast_dynamic-update-slice_fusion, s32[1024]{0:T(1024)S(1)} %pad_clamp_fusion), kind=kCustom, calls=%fused_computation | custom fusion | bytes 18350112 | tf_op jit(solution)/shard_map/gather | solution.py:64
  149.9 2.8 fusion.72
  152.7 3.2 fusion.77
  155.9 2.8 fusion.82
  164.8 2.0 fusion.4
  166.8 1.9 fusion.3
  168.7 1.9 fusion.2
  170.6 1.9 fusion.1
  172.6 1.9 fusion
  174.7 2.8 reduce.1
  178.7 33.3 %all_to_all.36 = bf16[32,2,8960]{2,1,0:T(2,128)(2,1)S(1)} all-to-all(bf16[32,2,8960]{2,1,0:T(2,128)(2,1)} %reshape.124), channel_id=1, replica_groups=mesh['dp'=8,'expert'=32] {'expert'}, dimensions={0} | all-to-all | bytes 2293760 | tf_op jit(solution)/shard_map/all_to_all | solution.py:52
  212.0 3.4 reshape.125
  215.4 2.9 copy.47
  218.3 11.6 %reduce-scatter.3.cloned.1.call-done = bf16[32,17920]{1,0:T(8,128)(2,1)} async-done(((bf16[256,17920]{1,0:T(8,128)(2,1)}), bf16[32,17920]{1,0:T(8,128)(2,1)}) %reduce-scatter.3.cloned.1.call-update) | async-done | bytes 1146896 | tf_op jit(solution)/shard_map/reduce_scatter | solution.py:101
  231.5 1.6 slice_dynamic-update-slice_fusion.8
  233.1 3.6 %copy-done.13 = bf16[1280,3584]{1,0:T(8,128)(2,1)} copy-done((bf16[1280,3584]{1,0:T(8,128)(2,1)}, bf16[1280,3584]{1,0:T(8,128)(2,1)S(1)}, u32[]{:S(2)}) %copy-start.13) | copy-done | bytes 9175064
  236.7 2.8 reduce.2
  240.6 10.2 %all-to-all-start.2 = ((bf16[32,2,8960]{2,1,0:T(2,128)(2,1)}), bf16[32,2,8960]{2,1,0:T(2,128)(2,1)S(1)}, u32[]{:S(2)}, u32[]{:S(2)}) async-start(bf16[32,2,8960]{2,1,0:T(2,128)(2,1)} %reshape.126), calls=%async_computation.3 | async-start | bytes 2293760 | tf_op jit(solution)/shard_map/all_to_all | solution.py:104
  250.9 2.9 slice_dynamic-update-slice_fusion.7
  253.8 3.0 slice_dynamic-update-slice_fusion.6
  256.7 2.9 slice_dynamic-update-slice_fusion.5
  259.6 18.9 %all-to-all-done.2 = bf16[32,2,8960]{2,1,0:T(2,128)(2,1)S(1)} async-done(((bf16[32,2,8960]{2,1,0:T(2,128)(2,1)}), bf16[32,2,8960]{2,1,0:T(2,128)(2,1)S(1)}, u32[]{:S(2)}, u32[]{:S(2)}) %all-to-all-start.2) | async-done | bytes 1146912 | tf_op jit(solution)/shard_map/all_to_all | solution.py:104
  278.6 3.4 reshape.127
  281.9 1.8 copy.46
  283.7 3.7 %all-gather.2.cloned.1.call-done = bf16[256,17920]{1,0:T(8,128)(2,1)} async-done(((bf16[32,17920]{1,0:T(8,128)(2,1)}), bf16[256,17920]{1,0:T(8,128)(2,1)}) %all-gather.2.cloned.1.call-update) | async-done | bytes 9175056 | tf_op jit(solution)/shard_map/all_gather | solution.py:103
  295.5 4.0 %fusion.10 = f32[1280,224]{0,1:T(8,128)} fusion(bf16[1280,3584]{1,0:T(8,128)(2,1)S(1)} %slice_dynamic-update-slice_fusion, bf16[1,224,3584]{2,1,0:T(8,128)(2,1)S(1)} %copy-done), kind=kOutput, calls=%fused_computation.30 | convolution fusion | flops 2055208960 | bytes 11927552 | tf_op jit(solution)/shard_map/dot_general | solution.py:107
  299.7 1.9 convolution_convert_fusion.9
  303.2 7.2 %fusion.7 = bf16[1,224,3584]{2,1,0:T(8,128)(2,1)} fusion(bf16[1280,224]{0,1:T(8,128)(2,1)S(1)} %multiply_convert_fusion.3, bf16[1280,3584]{1,0:T(8,128)(2,1)} %copy-done.14), kind=kOutput, calls=%fused_computation.17 | convolution fusion | flops 2056011776 | bytes 11354112 | tf_op jit(solution)/shard_map/dot_general | solution.py:114
  310.4 3.5 %fusion.6 = bf16[1,224,3584]{2,1,0:T(8,128)(2,1)} fusion(bf16[1280,3584]{1,0:T(8,128)(2,1)S(1)} %bitcast.127, f32[1280,224]{0,1:T(8,128)S(1)} %copy-done.18, f32[1280,224]{0,1:T(8,128)S(1)} %copy-done.7), kind=kOutput, calls=%fused_computation.16 | convolution fusion | flops 2057732096 | bytes 13074432 | tf_op jit(solution)/shard_map/dot_general | solution.py:116
  313.9 3.7 %fusion.5 = bf16[1,224,3584]{2,1,0:T(8,128)(2,1)} fusion(bf16[1280,3584]{1,0:T(8,128)(2,1)S(1)} %bitcast.127, f32[1280,224]{0,1:T(8,128)S(1)} %copy-done.7, f32[1280,224]{0,1:T(8,128)S(1)} %copy-done.18, f32[1280,224]{0,1:T(8,128)S(1)} %copy-done.5), kind=kOutput, calls=%fused_computation.15 | convolution fusion | flops 2058878976 | bytes 14221312 | tf_op jit(solution)/shard_map/dot_general | solution.py:115
  317.6 20.5 %reduce-scatter.5.cloned.1.call-done = bf16[16,3592]{1,0:T(8,128)(2,1)} async-done(((bf16[128,3592]{1,0:T(8,128)(2,1)}), bf16[16,3592]{1,0:T(8,128)(2,1)}) %reduce-scatter.5.cloned.1.call-update) | async-done | bytes 114960 | tf_op jit(solution)/shard_map/reduce_scatter | solution.py:126
  (116 shorter events, 37.1 us)
Async XLA Ops:
  7.2 157.7 %copy-start = (bf16[1,224,3584]{2,1,0:T(8,128)(2,1)S(1)}, bf16[1,224,3584]{2,1,0:T(8,128)(2,1)}, u32[]{:S(2)}) copy-start(bf16[1,224,3584]{2,1,0:T(8,128)(2,1)} %param.13) | copy-start | bytes 4816900
  7.2 2.0 copy-start.12
  9.7 1.0 copy-start.3
  15.2 11.9 %copy-start.15 = (f32[128,8]{0,1:T(8,128)S(1)}, f32[128,8]{0,1:T(8,128)}, u32[]{:S(2)}) copy-start(f32[128,8]{0,1:T(8,128)} %param.10) | copy-start | bytes 12292
  15.2 40.0 %all-to-all-start = ((bf16[32,2,8960]{2,1,0:T(2,128)(2,1)}), bf16[32,2,8960]{2,1,0:T(2,128)(2,1)S(1)}, u32[]{:S(2)}, u32[]{:S(2)}) async-start(bf16[32,2,8960]{2,1,0:T(2,128)(2,1)} %reshape.122), calls=%async_computation | async-start | bytes 2293760 | tf_op jit(solution)/shard_map/all_to_all | solution.py:50
  27.0 202.8 %reduce-scatter.3.cloned.1.call-start = ((), (), s32[]{:S(2)}) async-start(), calls=%async_computation.5 | async-start | bytes 10321920 | tf_op jit(solution)/shard_map/reduce_scatter | solution.py:101
  60.3 16.5 %collective-permute-start = (bf16[32,17920]{1,0:T(8,128)(2,1)S(1)}, bf16[32,17920]{1,0:T(8,128)(2,1)S(1)}, u32[]{:S(2)}, u32[]{:S(2)}) collective-permute-start(bf16[32,17920]{1,0:T(8,128)(2,1)S(1)} %bitcast.120), channel_id=1, source_target_pairs={{0,32},{32,64},{64,96},{96,128},{128,160},{160,192},{192,224},{224... | collective-permute-start | bytes 3440648 | tf_op jit(solution)/shard_map/ppermute | solution.py:59
  76.8 16.5 %copy-start.8 = (bf16[32,17920]{1,0:T(8,128)(2,1)}, bf16[32,17920]{1,0:T(8,128)(2,1)S(1)}, u32[]{:S(2)}) copy-start(bf16[32,17920]{1,0:T(8,128)(2,1)S(1)} %collective-permute-done) | copy-start | bytes 3440644
  76.8 16.5 %collective-permute-start.1 = (bf16[32,17920]{1,0:T(8,128)(2,1)S(1)}, bf16[32,17920]{1,0:T(8,128)(2,1)S(1)}, u32[]{:S(2)}, u32[]{:S(2)}) collective-permute-start(bf16[32,17920]{1,0:T(8,128)(2,1)S(1)} %collective-permute-done), channel_id=1, source_target_pairs={{0,32},{32,64},{64,96},{96,128},{128,160},{160,192},{192,224},{224... | collective-permute-start | bytes 3440648 | tf_op jit(solution)/shard_map/ppermute | solution.py:59
  76.8 16.5 %collective-permute-start.4 = (bf16[32,17920]{1,0:T(8,128)(2,1)S(1)}, bf16[32,17920]{1,0:T(8,128)(2,1)}, u32[]{:S(2)}, u32[]{:S(2)}) collective-permute-start(bf16[32,17920]{1,0:T(8,128)(2,1)S(1)} %bitcast.121), channel_id=1, source_target_pairs={{32,0},{64,32},{96,64},{128,96},{160,128},{192,160},{224,192},{0,2... | collective-permute-start | bytes 3440648 | tf_op jit(solution)/shard_map/ppermute | solution.py:61
  93.3 3.1 copy-start.10
  93.3 16.6 %collective-permute-start.2 = (bf16[32,17920]{1,0:T(8,128)(2,1)S(1)}, bf16[32,17920]{1,0:T(8,128)(2,1)}, u32[]{:S(2)}, u32[]{:S(2)}) collective-permute-start(bf16[32,17920]{1,0:T(8,128)(2,1)S(1)} %collective-permute-done.1), channel_id=1, source_target_pairs={{0,32},{32,64},{64,96},{96,128},{128,160},{160,192},{192,224},{224... | collective-permute-start | bytes 3440648 | tf_op jit(solution)/shard_map/ppermute | solution.py:59
  93.3 16.7 %collective-permute-start.5 = (bf16[32,17920]{1,0:T(8,128)(2,1)}, bf16[32,17920]{1,0:T(8,128)(2,1)}, u32[]{:S(2)}, u32[]{:S(2)}) collective-permute-start(bf16[32,17920]{1,0:T(8,128)(2,1)} %collective-permute-done.4), channel_id=1, source_target_pairs={{32,0},{64,32},{96,64},{128,96},{160,128},{192,160},{224,192},{0,2... | collective-permute-start | bytes 3440648 | tf_op jit(solution)/shard_map/ppermute | solution.py:61
  109.9 16.8 %collective-permute-start.3 = (bf16[32,17920]{1,0:T(8,128)(2,1)}, bf16[32,17920]{1,0:T(8,128)(2,1)}, u32[]{:S(2)}, u32[]{:S(2)}) collective-permute-start(bf16[32,17920]{1,0:T(8,128)(2,1)} %collective-permute-done.2), channel_id=1, source_target_pairs={{0,32},{32,64},{64,96},{96,128},{128,160},{160,192},{192,224},{224... | collective-permute-start | bytes 3440648 | tf_op jit(solution)/shard_map/ppermute | solution.py:59
  110.0 30.1 %collective-permute-start.6 = (bf16[32,17920]{1,0:T(8,128)(2,1)}, bf16[32,17920]{1,0:T(8,128)(2,1)S(1)}, u32[]{:S(2)}, u32[]{:S(2)}) collective-permute-start(bf16[32,17920]{1,0:T(8,128)(2,1)} %collective-permute-done.5), channel_id=1, source_target_pairs={{32,0},{64,32},{96,64},{128,96},{160,128},{192,160},{224,192},{0,2... | collective-permute-start | bytes 3440648 | tf_op jit(solution)/shard_map/ppermute | solution.py:61
  129.0 2.5 copy-start.11
  131.5 1.7 copy-start.9
  149.9 8.9 %copy-start.1 = (bf16[8,32,17920]{2,1,0:T(8,128)(2,1)S(1)}, bf16[8,32,17920]{2,1,0:T(8,128)(2,1)}, u32[]{:S(2)}) copy-start(bf16[8,32,17920]{2,1,0:T(8,128)(2,1)} %gather_fusion) | copy-start | bytes 27525124
  155.9 2.8 copy-start.16
  159.5 1.4 copy-start.17
  160.9 3.6 %copy-start.4 = (f32[1280,224]{0,1:T(8,128)}, f32[1280,224]{0,1:T(8,128)S(1)}, u32[]{:S(2)}) copy-start(f32[1280,224]{0,1:T(8,128)S(1)} %fusion.92) | copy-start | bytes 3440644
  164.5 2.3 copy-start.6
  174.5 112.9 %all-gather.2.cloned.1.call-start = ((), (), s32[]{:S(2)}) async-start(), calls=%async_computation.6 | async-start | bytes 10321920 | tf_op jit(solution)/shard_map/all_gather | solution.py:103
  233.1 3.6 %copy-start.13 = (bf16[1280,3584]{1,0:T(8,128)(2,1)}, bf16[1280,3584]{1,0:T(8,128)(2,1)S(1)}, u32[]{:S(2)}) copy-start(bf16[1280,3584]{1,0:T(8,128)(2,1)S(1)} %slice_dynamic-update-slice_fusion.8) | copy-start | bytes 27525124
  240.6 37.9 %all-to-all-start.2 = ((bf16[32,2,8960]{2,1,0:T(2,128)(2,1)}), bf16[32,2,8960]{2,1,0:T(2,128)(2,1)S(1)}, u32[]{:S(2)}, u32[]{:S(2)}) async-start(bf16[32,2,8960]{2,1,0:T(2,128)(2,1)} %reshape.126), calls=%async_computation.3 | async-start | bytes 2293760 | tf_op jit(solution)/shard_map/all_to_all | solution.py:104
  250.8 87.3 %reduce-scatter.5.cloned.1.call-start = ((), (), s32[]{:S(2)}) async-start(), calls=%async_computation.7 | async-start | bytes 1069056 | tf_op jit(solution)/shard_map/reduce_scatter | solution.py:126
  295.5 4.0 %copy-start.14 = (bf16[1280,3584]{1,0:T(8,128)(2,1)}, bf16[1280,3584]{1,0:T(8,128)(2,1)S(1)}, u32[]{:S(2)}) copy-start(bf16[1280,3584]{1,0:T(8,128)(2,1)S(1)} %slice_dynamic-update-slice_fusion) | copy-start | bytes 27525124
  299.6 1.9 copy-start.2
  303.1 7.2 %slice-start = ((s8[9175040]{0:T(1024)(128)(4,1)}), s8[786432]{0:T(1024)(128)(4,1)S(1)}, s32[]{:S(2)}) async-start(s8[9175040]{0:T(1024)(128)(4,1)} %bitcast.126), calls=%async_computation.8 | async-start | bytes 1572864
  303.2 7.2 %copy-start.7 = (f32[1280,224]{0,1:T(8,128)S(1)}, f32[1280,224]{0,1:T(8,128)}, u32[]{:S(2)}) copy-start(f32[1280,224]{0,1:T(8,128)} %copy-done.6) | copy-start | bytes 3440644
  303.2 7.2 %slice-start.1 = ((s8[9175040]{0:T(1024)(128)(4,1)}), s8[4194304]{0:T(1024)(128)(4,1)S(1)}, s32[]{:S(2)}) async-start(s8[9175040]{0:T(1024)(128)(4,1)} %bitcast.126), calls=%async_computation.9 | async-start | bytes 8388608
  303.2 7.2 %slice-start.2 = ((s8[9175040]{0:T(1024)(128)(4,1)}), s8[4194304]{0:T(1024)(128)(4,1)S(1)}, s32[]{:S(2)}) async-start(s8[9175040]{0:T(1024)(128)(4,1)} %bitcast.126), calls=%async_computation.10 | async-start | bytes 8388608
  303.2 7.2 %copy-start.18 = (f32[1280,224]{0,1:T(8,128)S(1)}, f32[1280,224]{0,1:T(8,128)}, u32[]{:S(2)}) copy-start(f32[1280,224]{0,1:T(8,128)} %fusion.10) | copy-start | bytes 3440644
  310.4 3.5 %copy-start.5 = (f32[1280,224]{0,1:T(8,128)S(1)}, f32[1280,224]{0,1:T(8,128)}, u32[]{:S(2)}) copy-start(f32[1280,224]{0,1:T(8,128)} %copy-done.4) | copy-start | bytes 3440644
Sparse Core Ops, SparseCore 0:
  174.6 55.1 reduce-scatter.2
  232.2 55.1 all-gather.1
  303.3 34.7 reduce-scatter.4
